TPU v7x, 32 devices: a whole 2x2x4 slice. The times are simulated.
32 devices in a mesh: tm: 8 (over z, y), col: 4 (over x, core).
Axes of the slice: x: 2, y: 2, z: 4, core: 2. Of those that a mesh axis runs over, the one named last changes fastest.
Arguments:
- observed: bfloat16 [16, 128, 512], P('tm', None, 'col'), may hold values from -6 to 6
- input_gain: float32 [512], P('col'), may hold values from 0.03 to 0.3
- persist: float32 [16, 512], P('tm', 'col'), may hold values from 0.5 to 1, as said below
- coupling: bfloat16 [16, 512, 512], P('tm', None, 'col'), may hold values from -0.02734375 to 0.02734375
- pattern: int32 [8, 8], replicated, may hold values 0 or 1
Outputs:
- filtered: float32 [16, 128, 512], P('tm', None, 'col')
- smoothed: float32 [16, 128, 512], P('tm', None, 'col')
Inputs may be any that keep to these rules, and one draw needn't show every extreme that they name: `persist`: persistence of each state component at each step.
All inputs are finite; a program needn't handle non-finite values.
Results may differ from a plain program's by a relative error of at most 0.0003.
Values may be sent and summed in bfloat16 or wider, within the bound.
No kernel may reach another device: no remote copies, remote signals or barrier semaphores. Data moves between devices by JAX's collectives and lax.ppermute only.
A program may use at most 64 MiB of HBM per device.

v0:
```python
import jax
import jax.numpy as jnp
from jax import lax
from jax.sharding import PartitionSpec as P


def passed_along(shard, axis, by):
    length = lax.axis_size(axis)
    pairs = [(i, i + by) for i in range(length) if 0 <= i + by < length]
    return lax.ppermute(shard, axis, pairs)


def matmul(left, right):
    return jnp.dot(left, right, precision=lax.Precision.HIGHEST, preferred_element_type=jnp.float32)


def advance(state, matrix):
    return matmul(lax.all_gather(state, "col", axis=1, tiled=True), matrix)


def smooth_step(later, state_full, state_part, cols_matrix, rows_matrix):
    predicted = matmul(state_full, cols_matrix)
    residual = later - predicted
    residual_full = lax.all_gather(residual, "col", axis=1, tiled=True)
    return state_part + matmul(residual_full, rows_matrix.T)


def local(observed, input_gain, persist, coupling, pattern):
    step_count = observed.shape[0]
    panels = observed.shape[1]
    state_width = coupling.shape[1]
    col_count = coupling.shape[2]
    block_count = pattern.shape[0]
    block_size = state_width // block_count
    col_pos = lax.axis_index("col")
    tm_pos = lax.axis_index("tm")
    time_block_groups = lax.axis_size("tm")
    first_col = col_pos * col_count
    pattern_real = pattern.astype(jnp.float32)
    row_ids = jnp.arange(state_width)
    col_ids = first_col + jnp.arange(col_count)
    block_labels = jnp.arange(block_count)
    row_hot = (row_ids[:, None] // block_size == block_labels[None, :]).astype(jnp.float32)
    col_hot = (col_ids[:, None] // block_size == block_labels[None, :]).astype(jnp.float32)
    mask_cols = matmul(matmul(row_hot, pattern_real), col_hot.T)
    mask_rows = matmul(matmul(col_hot, pattern_real), row_hot.T)
    diag_cols = (row_ids[:, None] == col_ids[None, :]).astype(jnp.float32)
    diag_rows = diag_cols.T
    trans_cols = (
        coupling.astype(jnp.float32) * mask_cols[None] + diag_cols[None] * persist[:, None, :]
    )
    rows_coupling = lax.all_to_all(coupling, "col", split_axis=1, concat_axis=2, tiled=True)
    trans_rows = (
        rows_coupling.astype(jnp.float32) * mask_rows[None] + diag_rows[None] * persist[:, :, None]
    )
    driven = input_gain[None, None, :] * observed.astype(jnp.float32)
    top_zeros = jnp.zeros((state_width, col_count), jnp.float32)
    state = jnp.concatenate([diag_cols, jnp.zeros((panels, col_count), jnp.float32)], axis=0)
    history = []
    for position in range(step_count):
        state = advance(state, trans_cols[position]) + jnp.concatenate(
            [top_zeros, driven[position]], axis=0
        )
        history.append(state)
    stacked_rows = jnp.stack(history)
    element = history[-1]
    saved = []
    stride = 1
    whole = lax.all_gather(element, "col", axis=1, tiled=True)
    whole_zeros = jnp.zeros((state_width, state_width), jnp.float32)
    while stride < time_block_groups:
        own_prod = whole[:state_width]
        saved.append(lax.dynamic_slice_in_dim(own_prod, first_col, col_count, 1))
        prior_values = passed_along(whole, "tm", stride)
        joined = matmul(prior_values, own_prod) + jnp.concatenate(
            [whole_zeros, whole[state_width:]], axis=0
        )
        whole = jnp.where(tm_pos >= stride, joined, whole)
        stride = stride * 2
    end_slice = lax.dynamic_slice_in_dim(whole[state_width:], first_col, col_count, 1)
    start_slice = passed_along(end_slice, "tm", 1)
    start_full = lax.all_gather(start_slice, "col", axis=1, tiled=True)
    filtered = (
        jnp.einsum(
            "bs,lsc->lbc",
            start_full,
            stacked_rows[:, :state_width],
            precision=lax.Precision.HIGHEST,
        )
        + stacked_rows[:, state_width:]
    )
    filtered_full = lax.all_gather(filtered, "col", axis=2, tiled=True)
    later = jnp.zeros((panels, col_count), jnp.float32)
    for position in range(step_count - 1, -1, -1):
        if position > 0:
            later = smooth_step(
                later,
                filtered_full[position - 1],
                filtered[position - 1],
                trans_cols[position],
                trans_rows[position],
            )
        else:
            later = smooth_step(
                later, start_full, start_slice, trans_cols[position], trans_rows[position]
            )
    offset = later
    from_next = passed_along(offset, "tm", -1)
    carried = jnp.where(tm_pos == time_block_groups - 1, filtered[step_count - 1], from_next)
    stride = 1
    for level_prod in saved:
        partial_value = matmul(carried, level_prod.T)
        shares = lax.psum_scatter(partial_value, "col", scatter_dimension=1, tiled=True)
        carried = carried + passed_along(shares, "tm", -stride)
        stride = stride * 2
    later = carried
    smoothed_list = [carried]
    position = 1
    later = smooth_step(
        later,
        filtered_full[position - 1],
        filtered[position - 1],
        trans_cols[position],
        trans_rows[position],
    )
    smoothed_list.append(later)
    smoothed = jnp.stack(smoothed_list[::-1])
    return (filtered, smoothed)


def solution(mesh):
    return jax.shard_map(
        local,
        mesh=mesh,
        in_specs=(P("tm", None, "col"), P("col"), P("tm", "col"), P("tm", None, "col"), P()),
        out_specs=(P("tm", None, "col"), P("tm", None, "col")),
        check_vma=False,
    )
```

profile of v0, /device:TPU:0, one launch (start us, length us, event | category | flops | bytes accessed | tf_op | source)
XLA Modules:
  0.0 347.9 jit_solution(4081061395193366817)
XLA Ops:
  7.3 0.7 concatenate.18
  8.1 1.0 fusion.16
  9.1 0.7 convert_multiply_fusion
  10.4 20.2 %all-gather.4.cloned.1.call-done = f32[640,512]{1,0:T(8,128)} async-done(((f32[640,128]{1,0:T(8,128)}), f32[640,512]{1,0:T(8,128)}) %all-gather.4.cloned.1.call-update) | async-done | bytes 1310736 | tf_op jit(solution)/shard_map/all_gather | solution.py:18
  30.6 3.2 convolution_add_fusion.3
  33.9 18.4 %all-gather.6.cloned.1.call-done = f32[640,512]{1,0:T(8,128)} async-done(((f32[640,128]{1,0:T(8,128)}), f32[640,512]{1,0:T(8,128)}) %all-gather.6.cloned.1.call-update) | async-done | bytes 1310736 | tf_op jit(solution)/shard_map/all_gather | solution.py:18
  52.3 3.2 convolution_add_fusion.2
  55.6 18.5 %all-gather.8.cloned.1.call-done = f32[640,512]{1,0:T(8,128)} async-done(((f32[640,128]{1,0:T(8,128)}), f32[640,512]{1,0:T(8,128)}) %all-gather.8.cloned.1.call-update) | async-done | bytes 1310736 | tf_op jit(solution)/shard_map/all_gather | solution.py:69
  74.1 3.4 collective-permute-start
  77.5 1.0 slice.85
  78.5 27.7 %collective-permute-done = f32[640,512]{1,0:T(8,128)S(1)} collective-permute-done((f32[640,512]{1,0:T(8,128)}, f32[640,512]{1,0:T(8,128)S(1)}, u32[]{:S(2)}, u32[]{:S(2)}) %collective-permute-start) | collective-permute-done | bytes 1310752 | tf_op jit(solution)/shard_map/ppermute | solution.py:10
  106.2 3.9 %fusion = f32[640,512]{1,0:T(8,128)S(1)} fusion(f32[640,512]{1,0:T(8,128)} %all-gather.8.cloned.1.call-done, f32[640,512]{1,0:T(8,128)S(1)} %collective-permute-done, f32[128,512]{1,0:T(8,128)S(1)} %slice.85, pred[]{:T(512)S(6)} %ge.11), kind=kOutput, calls=%fused_computation.2 | convolution fusion | flops 2013921280 | bytes 5242881 | tf_op jit(solution)/shard_map/dot_general | solution.py:14
  110.1 6.3 %collective-permute-start.1 = (f32[640,512]{1,0:T(8,128)S(1)}, f32[640,512]{1,0:T(8,128)}, u32[]{:S(2)}, u32[]{:S(2)}) collective-permute-start(f32[640,512]{1,0:T(8,128)S(1)} %fusion), channel_id=1, source_target_pairs={{0,8},{4,12},{8,16},{12,20},{16,24},{20,28},{1,9},{5,13},{9,17},{1... | collective-permute-start | bytes 3932168 | tf_op jit(solution)/shard_map/ppermute | solution.py:10
  116.5 26.5 %collective-permute-done.1 = f32[640,512]{1,0:T(8,128)} collective-permute-done((f32[640,512]{1,0:T(8,128)S(1)}, f32[640,512]{1,0:T(8,128)}, u32[]{:S(2)}, u32[]{:S(2)}) %collective-permute-start.1) | collective-permute-done | bytes 1310752 | tf_op jit(solution)/shard_map/ppermute | solution.py:10
  142.9 3.6 %fusion.1 = f32[640,512]{1,0:T(8,128)S(1)} fusion(f32[640,512]{1,0:T(8,128)S(1)} %fusion, f32[640,512]{1,0:T(8,128)} %collective-permute-done.1, f32[128,512]{1,0:T(8,128)S(1)} %slice.87, pred[]{:T(512)S(6)} %ge.10), kind=kOutput, calls=%fused_computation.3 | convolution fusion | flops 2013921280 | bytes 5242881 | tf_op jit(solution)/shard_map/dot_general | solution.py:14
  146.5 6.5 %collective-permute-start.2 = (f32[640,512]{1,0:T(8,128)S(1)}, f32[640,512]{1,0:T(8,128)}, u32[]{:S(2)}, u32[]{:S(2)}) collective-permute-start(f32[640,512]{1,0:T(8,128)S(1)} %fusion.1), channel_id=1, source_target_pairs={{0,16},{4,20},{8,24},{12,28},{1,17},{5,21},{9,25},{13,29},{2,18},{... | collective-permute-start | bytes 3932168 | tf_op jit(solution)/shard_map/ppermute | solution.py:10
  153.0 1.0 copy.18
  154.0 3.4 all-to-all-start
  157.6 1.1 fusion.15
  158.7 0.7 fusion.18
  159.5 3.9 %all-to-all-done = bf16[2,512,128]{2,0,1:T(2,128)(2,1)S(1)} async-done(((bf16[2,512,128]{2,0,1:T(2,128)(2,1)}), bf16[2,512,128]{2,0,1:T(2,128)(2,1)S(1)}, u32[]{:S(2)}, u32[]{:S(2)}) %all-to-all-start) | async-done | bytes 262176 | tf_op jit(solution)/shard_map/all_to_all | solution.py:52
  163.4 0.8 convert_bitcast_fusion
  164.2 2.0 copy.20
  166.3 12.4 %collective-permute-done.2 = f32[640,512]{1,0:T(8,128)} collective-permute-done((f32[640,512]{1,0:T(8,128)S(1)}, f32[640,512]{1,0:T(8,128)}, u32[]{:S(2)}, u32[]{:S(2)}) %collective-permute-start.2) | collective-permute-done | bytes 1310752 | tf_op jit(solution)/shard_map/ppermute | solution.py:10
  178.7 3.6 %fusion.39 = f32[640,512]{1,0:T(8,128)S(1)} fusion(f32[640,512]{1,0:T(8,128)} %collective-permute-done.2, f32[640,512]{1,0:T(8,128)S(1)} %fusion.1), kind=kOutput, calls=%fused_computation.80 | convolution fusion | flops 2013265920 | bytes 3670016 | tf_op jit(solution)/shard_map/dot_general | solution.py:14
  182.3 2.6 collective-permute-start.3
  185.1 1.8 collective-permute-done.3
  186.9 5.9 %all_gather.27 = f32[128,512]{1,0:T(8,128)S(1)} all-gather(f32[128,128]{1,0:T(8,128)S(1)} %collective-permute-done.3), channel_id=1, replica_groups=mesh['tm'=8,'col'=4] {'col'}, dimensions={1}, use_global_device_ids=true | all-gather | bytes 327680 | tf_op jit(solution)/shard_map/all_gather | solution.py:82
  193.3 7.3 %all_gather.28 = f32[2,128,512]{2,1,0:T(8,128)S(1)} all-gather(f32[2,128,128]{2,1,0:T(8,128)S(1)} %fusion.2), channel_id=1, replica_groups=mesh['tm'=8,'col'=4] {'col'}, dimensions={2}, use_global_device_ids=true | all-gather | bytes 655360 | tf_op jit(solution)/shard_map/all_gather | solution.py:92
  200.9 5.9 %all_gather.29 = f32[128,512]{1,0:T(8,128)S(1)} all-gather(f32[128,128]{1,0:T(8,128)S(1)} %get-tuple-element.6), channel_id=1, replica_groups=mesh['tm'=8,'col'=4] {'col'}, dimensions={1}, use_global_device_ids=true | all-gather | bytes 327680 | tf_op jit(solution)/shard_map/all_gather | solution.py:24
  207.6 5.9 %all_gather.30 = f32[128,512]{1,0:T(8,128)S(1)} all-gather(f32[128,128]{1,0:T(8,128)S(1)} %convolution_subtract_fusion), channel_id=1, replica_groups=mesh['tm'=8,'col'=4] {'col'}, dimensions={1}, use_global_device_ids=true | all-gather | bytes 327680 | tf_op jit(solution)/shard_map/all_gather | solution.py:24
  213.8 1.3 collective-permute-start.4
  215.1 1.3 slice.84
  216.4 32.3 %collective-permute-done.4 = f32[128,128]{1,0:T(8,128)S(1)} collective-permute-done((f32[128,128]{1,0:T(8,128)S(1)}, f32[128,128]{1,0:T(8,128)S(1)}, u32[]{:S(2)}, u32[]{:S(2)}) %collective-permute-start.4) | collective-permute-done | bytes 65568 | tf_op jit(solution)/shard_map/ppermute | solution.py:10
  248.7 1.1 fusion.13
  249.9 22.4 %reduce-scatter.4.cloned.1.call-done = f32[128,128]{1,0:T(8,128)} async-done(((f32[128,512]{1,0:T(8,128)}), f32[128,128]{1,0:T(8,128)}) %reduce-scatter.4.cloned.1.call-update) | async-done | bytes 65552 | tf_op jit(solution)/shard_map/reduce_scatter | solution.py:113
  272.2 1.3 collective-permute-start.5
  273.6 5.0 %collective-permute-done.5 = f32[128,128]{1,0:T(8,128)S(1)} collective-permute-done((f32[128,128]{1,0:T(8,128)}, f32[128,128]{1,0:T(8,128)S(1)}, u32[]{:S(2)}, u32[]{:S(2)}) %collective-permute-start.5) | collective-permute-done | bytes 65568 | tf_op jit(solution)/shard_map/ppermute | solution.py:10
  278.6 1.1 fusion.11
  279.8 20.2 %reduce-scatter.6.cloned.1.call-done = f32[128,128]{1,0:T(8,128)} async-done(((f32[128,512]{1,0:T(8,128)}), f32[128,128]{1,0:T(8,128)}) %reduce-scatter.6.cloned.1.call-update) | async-done | bytes 65552 | tf_op jit(solution)/shard_map/reduce_scatter | solution.py:113
  299.9 1.3 collective-permute-start.6
  301.3 5.0 %collective-permute-done.6 = f32[128,128]{1,0:T(8,128)S(1)} collective-permute-done((f32[128,128]{1,0:T(8,128)}, f32[128,128]{1,0:T(8,128)S(1)}, u32[]{:S(2)}, u32[]{:S(2)}) %collective-permute-start.6) | collective-permute-done | bytes 65568 | tf_op jit(solution)/shard_map/ppermute | solution.py:10
  306.3 1.1 fusion.9
  307.4 19.3 %reduce-scatter.8.cloned.1.call-done = f32[128,128]{1,0:T(8,128)} async-done(((f32[128,512]{1,0:T(8,128)}), f32[128,128]{1,0:T(8,128)}) %reduce-scatter.8.cloned.1.call-update) | async-done | bytes 65552 | tf_op jit(solution)/shard_map/reduce_scatter | solution.py:113
  326.7 1.3 collective-permute-start.7
  328.0 6.3 %collective-permute-done.7 = f32[128,128]{1,0:T(8,128)S(1)} collective-permute-done((f32[128,128]{1,0:T(8,128)}, f32[128,128]{1,0:T(8,128)S(1)}, u32[]{:S(2)}, u32[]{:S(2)}) %collective-permute-start.7) | collective-permute-done | bytes 65568 | tf_op jit(solution)/shard_map/ppermute | solution.py:10
  334.3 5.8 %all_gather.31 = f32[128,512]{1,0:T(8,128)S(1)} all-gather(f32[128,128]{1,0:T(8,128)S(1)} %get-tuple-element.2), channel_id=1, replica_groups=mesh['tm'=8,'col'=4] {'col'}, dimensions={1}, use_global_device_ids=true | all-gather | bytes 327680 | tf_op jit(solution)/shard_map/all_gather | solution.py:24
  340.4 0.7 pad_maximum_fusion.1
  (60 shorter events, 3.9 us)
Async XLA Ops:
  7.2 2.0 copy-start.9
  7.2 3.1 copy-start.10
  7.2 3.1 copy-start.6
  7.2 23.4 %all-gather.4.cloned.1.call-start = ((), (), s32[]{:S(2)}) async-start(), calls=%async_computation.4 | async-start | bytes 1638400 | tf_op jit(solution)/shard_map/all_gather | solution.py:18
  8.1 44.3 %all-gather.6.cloned.1.call-start = ((), (), s32[]{:S(2)}) async-start(), calls=%async_computation.5 | async-start | bytes 1638400 | tf_op jit(solution)/shard_map/all_gather | solution.py:18
  33.9 40.2 %all-gather.8.cloned.1.call-start = ((), (), s32[]{:S(2)}) async-start(), calls=%async_computation.6 | async-start | bytes 1638400 | tf_op jit(solution)/shard_map/all_gather | solution.py:69
  74.1 32.1 %collective-permute-start = (f32[640,512]{1,0:T(8,128)}, f32[640,512]{1,0:T(8,128)S(1)}, u32[]{:S(2)}, u32[]{:S(2)}) collective-permute-start(f32[640,512]{1,0:T(8,128)} %all-gather.8.cloned.1.call-done), channel_id=1, source_target_pairs={{0,4},{4,8},{8,12},{12,16},{16,20},{20,24},{24,28},{1,5},{5,9},{9,... | collective-permute-start | bytes 3932168 | tf_op jit(solution)/shard_map/ppermute | solution.py:10
  110.1 32.8 %collective-permute-start.1 = (f32[640,512]{1,0:T(8,128)S(1)}, f32[640,512]{1,0:T(8,128)}, u32[]{:S(2)}, u32[]{:S(2)}) collective-permute-start(f32[640,512]{1,0:T(8,128)S(1)} %fusion), channel_id=1, source_target_pairs={{0,8},{4,12},{8,16},{12,20},{16,24},{20,28},{1,9},{5,13},{9,17},{1... | collective-permute-start | bytes 3932168 | tf_op jit(solution)/shard_map/ppermute | solution.py:10
  116.4 41.0 %copy-start.11 = (s32[8,8]{1,0:T(8,128)S(1)}, s32[8,8]{1,0:T(8,128)}, u32[]{:S(2)}) copy-start(s32[8,8]{1,0:T(8,128)} %param.9) | copy-start | bytes 772
  146.5 32.2 %collective-permute-start.2 = (f32[640,512]{1,0:T(8,128)S(1)}, f32[640,512]{1,0:T(8,128)}, u32[]{:S(2)}, u32[]{:S(2)}) collective-permute-start(f32[640,512]{1,0:T(8,128)S(1)} %fusion.1), channel_id=1, source_target_pairs={{0,16},{4,20},{8,24},{12,28},{1,17},{5,21},{9,25},{13,29},{2,18},{... | collective-permute-start | bytes 3932168 | tf_op jit(solution)/shard_map/ppermute | solution.py:10
  154.0 9.4 %all-to-all-start = ((bf16[2,512,128]{2,0,1:T(2,128)(2,1)}), bf16[2,512,128]{2,0,1:T(2,128)(2,1)S(1)}, u32[]{:S(2)}, u32[]{:S(2)}) async-start(bf16[2,512,128]{2,0,1:T(2,128)(2,1)} %copy.18), calls=%async_computation | async-start | bytes 524288 | tf_op jit(solution)/shard_map/all_to_all | solution.py:52
  157.4 114.9 %reduce-scatter.4.cloned.1.call-start = ((), (), s32[]{:S(2)}) async-start(), calls=%async_computation.7 | async-start | bytes 327680 | tf_op jit(solution)/shard_map/reduce_scatter | solution.py:113
  166.3 18.7 %copy-start.7 = (f32[128,512]{0,1:T(8,128)S(1)}, f32[128,512]{0,1:T(8,128)}, u32[]{:S(2)}) copy-start(f32[128,512]{0,1:T(8,128)} %fusion.15) | copy-start | bytes 786436
  166.3 18.7 %copy-start.8 = (f32[128,512]{0,1:T(8,128)S(1)}, f32[128,512]{0,1:T(8,128)}, u32[]{:S(2)}) copy-start(f32[128,512]{0,1:T(8,128)} %fusion.18) | copy-start | bytes 786436
  182.3 2.7 copy-start.5
  182.3 10.5 %copy-start = (f32[640,128]{1,0:T(8,128)S(1)}, f32[640,128]{1,0:T(8,128)}, u32[]{:S(2)}) copy-start(f32[640,128]{1,0:T(8,128)} %convolution_add_fusion.3) | copy-start | bytes 983044
  182.3 10.5 %copy-start.1 = (f32[640,128]{1,0:T(8,128)S(1)}, f32[640,128]{1,0:T(8,128)}, u32[]{:S(2)}) copy-start(f32[640,128]{1,0:T(8,128)} %convolution_add_fusion.2) | copy-start | bytes 983044
  182.3 4.5 %collective-permute-start.3 = (f32[128,128]{1,0:T(8,128)S(1)}, f32[128,128]{1,0:T(8,128)S(1)}, u32[]{:S(2)}, u32[]{:S(2)}) collective-permute-start(f32[128,128]{1,0:T(8,128)S(1)} %fusion.22), channel_id=1, source_target_pairs={{0,4},{4,8},{8,12},{12,16},{16,20},{20,24},{24,28},{1,5},{5,9},{9,... | collective-permute-start | bytes 196616 | tf_op jit(solution)/shard_map/ppermute | solution.py:10
  185.1 28.4 %copy-start.2 = (f32[2,128,512]{1,2,0:T(8,128)}, f32[2,128,512]{1,2,0:T(8,128)S(1)}, u32[]{:S(2)}) copy-start(f32[2,128,512]{1,2,0:T(8,128)S(1)} %fusion.6) | copy-start | bytes 1572868
  193.2 146.8 %copy-start.4 = (f32[2,128,128]{2,1,0:T(8,128)}, f32[2,128,128]{2,1,0:T(8,128)S(1)}, u32[]{:S(2)}) copy-start(f32[2,128,128]{2,1,0:T(8,128)S(1)} %fusion.2) | copy-start | bytes 393220
  213.8 34.9 %collective-permute-start.4 = (f32[128,128]{1,0:T(8,128)S(1)}, f32[128,128]{1,0:T(8,128)S(1)}, u32[]{:S(2)}, u32[]{:S(2)}) collective-permute-start(f32[128,128]{1,0:T(8,128)S(1)} %convolution_add_fusion.5), channel_id=1, source_target_pairs={{4,0},{8,4},{12,8},{16,12},{20,16},{24,20},{28,24},{5,1},{9,5},{13... | collective-permute-start | bytes 196616 | tf_op jit(solution)/shard_map/ppermute | solution.py:10
  249.8 50.1 %reduce-scatter.6.cloned.1.call-start = ((), (), s32[]{:S(2)}) async-start(), calls=%async_computation.8 | async-start | bytes 327680 | tf_op jit(solution)/shard_map/reduce_scatter | solution.py:113
  272.2 6.4 %collective-permute-start.5 = (f32[128,128]{1,0:T(8,128)}, f32[128,128]{1,0:T(8,128)S(1)}, u32[]{:S(2)}, u32[]{:S(2)}) collective-permute-start(f32[128,128]{1,0:T(8,128)} %reduce-scatter.4.cloned.1.call-done), channel_id=1, source_target_pairs={{4,0},{8,4},{12,8},{16,12},{20,16},{24,20},{28,24},{5,1},{9,5},{13... | collective-permute-start | bytes 196616 | tf_op jit(solution)/shard_map/ppermute | solution.py:10
  279.7 47.0 %reduce-scatter.8.cloned.1.call-start = ((), (), s32[]{:S(2)}) async-start(), calls=%async_computation.9 | async-start | bytes 327680 | tf_op jit(solution)/shard_map/reduce_scatter | solution.py:113
  299.9 6.4 %collective-permute-start.6 = (f32[128,128]{1,0:T(8,128)}, f32[128,128]{1,0:T(8,128)S(1)}, u32[]{:S(2)}, u32[]{:S(2)}) collective-permute-start(f32[128,128]{1,0:T(8,128)} %reduce-scatter.6.cloned.1.call-done), channel_id=1, source_target_pairs={{8,0},{12,4},{16,8},{20,12},{24,16},{28,20},{9,1},{13,5},{17,9},{2... | collective-permute-start | bytes 196616 | tf_op jit(solution)/shard_map/ppermute | solution.py:10
  301.3 38.7 %copy-start.3 = (f32[2,128,512]{1,2,0:T(8,128)S(1)}, f32[2,128,512]{1,2,0:T(8,128)}, u32[]{:S(2)}) copy-start(f32[2,128,512]{1,2,0:T(8,128)} %copy-done.2) | copy-start | bytes 1572868
  326.7 7.6 %collective-permute-start.7 = (f32[128,128]{1,0:T(8,128)}, f32[128,128]{1,0:T(8,128)S(1)}, u32[]{:S(2)}, u32[]{:S(2)}) collective-permute-start(f32[128,128]{1,0:T(8,128)} %reduce-scatter.8.cloned.1.call-done), channel_id=1, source_target_pairs={{16,0},{20,4},{24,8},{28,12},{17,1},{21,5},{25,9},{29,13},{18,2},{... | collective-permute-start | bytes 196616 | tf_op jit(solution)/shard_map/ppermute | solution.py:10
Sparse Core Ops, SparseCore 0:
  9.6 21.0 all-gather.3
  34.0 18.3 all-gather.5
  55.7 18.3 all-gather.7
  249.9 22.2 reduce-scatter.3
  279.8 20.0 reduce-scatter.5
  307.5 19.1 reduce-scatter.7
where the time goes:
time: 349 us; the launch traced here: 348 us
  waiting for transfers between devices  240 us (69%)
  blocking collectives  30.7 us (9%)
  starting transfers between devices  27.6 us (8%)
  matrix products  25.9 us (7%)
  between operations  14.5 us (4%)
  local copies, waits for them, and re-layouts  6.3 us (2%)
    ppermute x8, waiting for transfers between devices, passed_along(): return lax.ppermute(shard, axis, pairs)  117 us
    reduce_scatter x3, waiting for transfers between devices, local(): lax.psum_scatter(partial_value, 'col', scatter_dimension=1, tiled=True)  61.8 us
    all_gather x2, waiting for transfers between devices, advance(): return matmul(lax.all_gather(state, 'col', axis=1, tiled=True), matrix)  38.7 us
    dot_general x17, matrix products, matmul(): jnp.dot(left, right, precision=lax.Precision.HIGHEST, preferred_element_t...  25.4 us
    ppermute x8, starting transfers between devices, passed_along(): return lax.ppermute(shard, axis, pairs)  24 us
    all_gather x1, waiting for transfers between devices, local(): whole = lax.all_gather(element, 'col', axis=1, tiled=True)  18.5 us
    all_gather x3, blocking collectives, smooth_step(): residual_full = lax.all_gather(residual, 'col', axis=1, tiled=True)  17.5 us
    all_gather x1, blocking collectives, local(): filtered_full = lax.all_gather(filtered, 'col', axis=2, tiled=True)  7.28 us
  transfers between devices with their start and end apart: 15, of which 15 were waited for; matrix products, arithmetic and copies ran while one was open for 3% of the time, Pallas kernels for 0%

commit v1 on v0

--- a/solution.py
+++ b/solution.py
@@ -49,7 +49,10 @@
     trans_cols = (
         coupling.astype(jnp.float32) * mask_cols[None] + diag_cols[None] * persist[:, None, :]
     )
-    rows_coupling = lax.all_to_all(coupling, "col", split_axis=1, concat_axis=2, tiled=True)
+    rows_coupling = jnp.concatenate(
+        lax.all_to_all(jnp.stack(jnp.split(coupling, lax.axis_size("col"), axis=1)), "col", 0, 0),
+        axis=2,
+    )
     trans_rows = (
         rows_coupling.astype(jnp.float32) * mask_rows[None] + diag_rows[None] * persist[:, :, None]
     )

time: 349 us -> 349 us (level)
  no operation moved by 1% of the time
where the time goes in v1:
time: 349 us; the launch traced here: 348 us
  waiting for transfers between devices  239 us (68%)
  blocking collectives  30.7 us (9%)
  starting transfers between devices  27.6 us (8%)
  matrix products  26.4 us (8%)
  between operations  14.5 us (4%)
  local copies, waits for them, and re-layouts  6.08 us (2%)
    ppermute x8, waiting for transfers between devices, passed_along(): return lax.ppermute(shard, axis, pairs)  117 us
    reduce_scatter x3, waiting for transfers between devices, local(): lax.psum_scatter(partial_value, 'col', scatter_dimension=1, tiled=True)  61.8 us
    all_gather x2, waiting for transfers between devices, advance(): return matmul(lax.all_gather(state, 'col', axis=1, tiled=True), matrix)  38.7 us
    dot_general x17, matrix products, matmul(): jnp.dot(left, right, precision=lax.Precision.HIGHEST, preferred_element_t...  26 us
    ppermute x8, starting transfers between devices, passed_along(): return lax.ppermute(shard, axis, pairs)  24 us
    all_gather x1, waiting for transfers between devices, local(): whole = lax.all_gather(element, 'col', axis=1, tiled=True)  18.5 us
    all_gather x3, blocking collectives, smooth_step(): residual_full = lax.all_gather(residual, 'col', axis=1, tiled=True)  17.5 us
    all_gather x1, blocking collectives, local(): filtered_full = lax.all_gather(filtered, 'col', axis=2, tiled=True)  7.28 us
  transfers between devices with their start and end apart: 15, of which 15 were waited for; matrix products, arithmetic and copies ran while one was open for 3% of the time, Pallas kernels for 0%

profile of v1, /device:TPU:0, one launch (start us, length us, event | category | flops | bytes accessed | tf_op | source)
XLA Modules:
  0.0 347.8 jit_solution(642039474976971426)
XLA Ops:
  7.3 0.7 concatenate.18
  8.1 1.0 fusion.16
  9.1 0.7 convert_multiply_fusion
  10.4 20.2 %all-gather.4.cloned.1.call-done = f32[640,512]{1,0:T(8,128)} async-done(((f32[640,128]{1,0:T(8,128)}), f32[640,512]{1,0:T(8,128)}) %all-gather.4.cloned.1.call-update) | async-done | bytes 1310736 | tf_op jit(solution)/shard_map/all_gather | solution.py:18
  30.6 3.2 convolution_add_fusion.3
  33.9 18.4 %all-gather.6.cloned.1.call-done = f32[640,512]{1,0:T(8,128)} async-done(((f32[640,128]{1,0:T(8,128)}), f32[640,512]{1,0:T(8,128)}) %all-gather.6.cloned.1.call-update) | async-done | bytes 1310736 | tf_op jit(solution)/shard_map/all_gather | solution.py:18
  52.4 3.2 convolution_add_fusion.2
  55.6 18.5 %all-gather.8.cloned.1.call-done = f32[640,512]{1,0:T(8,128)} async-done(((f32[640,128]{1,0:T(8,128)}), f32[640,512]{1,0:T(8,128)}) %all-gather.8.cloned.1.call-update) | async-done | bytes 1310736 | tf_op jit(solution)/shard_map/all_gather | solution.py:72
  74.1 3.4 collective-permute-start
  77.5 1.0 slice.85
  78.5 27.7 %collective-permute-done = f32[640,512]{1,0:T(8,128)S(1)} collective-permute-done((f32[640,512]{1,0:T(8,128)}, f32[640,512]{1,0:T(8,128)S(1)}, u32[]{:S(2)}, u32[]{:S(2)}) %collective-permute-start) | collective-permute-done | bytes 1310752 | tf_op jit(solution)/shard_map/ppermute | solution.py:10
  106.2 3.9 %fusion = f32[640,512]{1,0:T(8,128)S(1)} fusion(f32[640,512]{1,0:T(8,128)} %all-gather.8.cloned.1.call-done, f32[640,512]{1,0:T(8,128)S(1)} %collective-permute-done, f32[128,512]{1,0:T(8,128)S(1)} %slice.85, pred[]{:T(512)S(6)} %ge.11), kind=kOutput, calls=%fused_computation.2 | convolution fusion | flops 2013921280 | bytes 5242881 | tf_op jit(solution)/shard_map/dot_general | solution.py:14
  110.1 6.3 %collective-permute-start.1 = (f32[640,512]{1,0:T(8,128)S(1)}, f32[640,512]{1,0:T(8,128)}, u32[]{:S(2)}, u32[]{:S(2)}) collective-permute-start(f32[640,512]{1,0:T(8,128)S(1)} %fusion), channel_id=1, source_target_pairs={{0,8},{4,12},{8,16},{12,20},{16,24},{20,28},{1,9},{5,13},{9,17},{1... | collective-permute-start | bytes 3932168 | tf_op jit(solution)/shard_map/ppermute | solution.py:10
  116.4 26.5 %collective-permute-done.1 = f32[640,512]{1,0:T(8,128)} collective-permute-done((f32[640,512]{1,0:T(8,128)S(1)}, f32[640,512]{1,0:T(8,128)}, u32[]{:S(2)}, u32[]{:S(2)}) %collective-permute-start.1) | collective-permute-done | bytes 1310752 | tf_op jit(solution)/shard_map/ppermute | solution.py:10
  142.8 3.6 %fusion.1 = f32[640,512]{1,0:T(8,128)S(1)} fusion(f32[640,512]{1,0:T(8,128)S(1)} %fusion, f32[640,512]{1,0:T(8,128)} %collective-permute-done.1, f32[128,512]{1,0:T(8,128)S(1)} %slice.87, pred[]{:T(512)S(6)} %ge.10), kind=kOutput, calls=%fused_computation.3 | convolution fusion | flops 2013921280 | bytes 5242881 | tf_op jit(solution)/shard_map/dot_general | solution.py:14
  146.4 6.5 %collective-permute-start.2 = (f32[640,512]{1,0:T(8,128)S(1)}, f32[640,512]{1,0:T(8,128)}, u32[]{:S(2)}, u32[]{:S(2)}) collective-permute-start(f32[640,512]{1,0:T(8,128)S(1)} %fusion.1), channel_id=1, source_target_pairs={{0,16},{4,20},{8,24},{12,28},{1,17},{5,21},{9,25},{13,29},{2,18},{... | collective-permute-start | bytes 3932168 | tf_op jit(solution)/shard_map/ppermute | solution.py:10
  153.6 0.9 copy.27
  154.5 1.0 copy.28
  155.8 0.7 pad_maximum_fusion
  156.5 3.4 all-to-all-start
  160.0 0.9 fusion.24
  160.8 1.1 fusion.15
  161.9 0.7 fusion.18
  162.6 3.2 all-to-all-done
  166.0 12.6 %collective-permute-done.2 = f32[640,512]{1,0:T(8,128)} collective-permute-done((f32[640,512]{1,0:T(8,128)S(1)}, f32[640,512]{1,0:T(8,128)}, u32[]{:S(2)}, u32[]{:S(2)}) %collective-permute-start.2) | collective-permute-done | bytes 1310752 | tf_op jit(solution)/shard_map/ppermute | solution.py:10
  178.6 3.5 %fusion.39 = f32[640,512]{1,0:T(8,128)S(1)} fusion(f32[640,512]{1,0:T(8,128)} %collective-permute-done.2, f32[640,512]{1,0:T(8,128)S(1)} %fusion.1), kind=kOutput, calls=%fused_computation.81 | convolution fusion | flops 2013265920 | bytes 3670016 | tf_op jit(solution)/shard_map/dot_general | solution.py:14
  182.2 2.6 collective-permute-start.3
  184.9 1.8 collective-permute-done.3
  186.7 5.9 %all_gather.27 = f32[128,512]{1,0:T(8,128)S(1)} all-gather(f32[128,128]{1,0:T(8,128)S(1)} %collective-permute-done.3), channel_id=1, replica_groups=mesh['tm'=8,'col'=4] {'col'}, dimensions={1}, use_global_device_ids=true | all-gather | bytes 327680 | tf_op jit(solution)/shard_map/all_gather | solution.py:85
  193.1 7.3 %all_gather.28 = f32[2,128,512]{2,1,0:T(8,128)S(1)} all-gather(f32[2,128,128]{2,1,0:T(8,128)S(1)} %fusion.2), channel_id=1, replica_groups=mesh['tm'=8,'col'=4] {'col'}, dimensions={2}, use_global_device_ids=true | all-gather | bytes 655360 | tf_op jit(solution)/shard_map/all_gather | solution.py:95
  200.8 5.9 %all_gather.29 = f32[128,512]{1,0:T(8,128)S(1)} all-gather(f32[128,128]{1,0:T(8,128)S(1)} %get-tuple-element.10), channel_id=1, replica_groups=mesh['tm'=8,'col'=4] {'col'}, dimensions={1}, use_global_device_ids=true | all-gather | bytes 327680 | tf_op jit(solution)/shard_map/all_gather | solution.py:24
  207.4 5.9 %all_gather.30 = f32[128,512]{1,0:T(8,128)S(1)} all-gather(f32[128,128]{1,0:T(8,128)S(1)} %convolution_subtract_fusion), channel_id=1, replica_groups=mesh['tm'=8,'col'=4] {'col'}, dimensions={1}, use_global_device_ids=true | all-gather | bytes 327680 | tf_op jit(solution)/shard_map/all_gather | solution.py:24
  213.7 1.3 collective-permute-start.4
  215.0 1.3 slice.84
  216.3 32.3 %collective-permute-done.4 = f32[128,128]{1,0:T(8,128)S(1)} collective-permute-done((f32[128,128]{1,0:T(8,128)S(1)}, f32[128,128]{1,0:T(8,128)S(1)}, u32[]{:S(2)}, u32[]{:S(2)}) %collective-permute-start.4) | collective-permute-done | bytes 65568 | tf_op jit(solution)/shard_map/ppermute | solution.py:10
  248.6 1.1 fusion.13
  249.8 22.4 %reduce-scatter.4.cloned.1.call-done = f32[128,128]{1,0:T(8,128)} async-done(((f32[128,512]{1,0:T(8,128)}), f32[128,128]{1,0:T(8,128)}) %reduce-scatter.4.cloned.1.call-update) | async-done | bytes 65552 | tf_op jit(solution)/shard_map/reduce_scatter | solution.py:116
  272.1 1.3 collective-permute-start.5
  273.5 5.0 %collective-permute-done.5 = f32[128,128]{1,0:T(8,128)S(1)} collective-permute-done((f32[128,128]{1,0:T(8,128)}, f32[128,128]{1,0:T(8,128)S(1)}, u32[]{:S(2)}, u32[]{:S(2)}) %collective-permute-start.5) | collective-permute-done | bytes 65568 | tf_op jit(solution)/shard_map/ppermute | solution.py:10
  278.5 1.1 fusion.11
  279.7 20.2 %reduce-scatter.6.cloned.1.call-done = f32[128,128]{1,0:T(8,128)} async-done(((f32[128,512]{1,0:T(8,128)}), f32[128,128]{1,0:T(8,128)}) %reduce-scatter.6.cloned.1.call-update) | async-done | bytes 65552 | tf_op jit(solution)/shard_map/reduce_scatter | solution.py:116
  299.8 1.3 collective-permute-start.6
  301.2 5.0 %collective-permute-done.6 = f32[128,128]{1,0:T(8,128)S(1)} collective-permute-done((f32[128,128]{1,0:T(8,128)}, f32[128,128]{1,0:T(8,128)S(1)}, u32[]{:S(2)}, u32[]{:S(2)}) %collective-permute-start.6) | collective-permute-done | bytes 65568 | tf_op jit(solution)/shard_map/ppermute | solution.py:10
  306.2 1.1 fusion.9
  307.3 19.3 %reduce-scatter.8.cloned.1.call-done = f32[128,128]{1,0:T(8,128)} async-done(((f32[128,512]{1,0:T(8,128)}), f32[128,128]{1,0:T(8,128)}) %reduce-scatter.8.cloned.1.call-update) | async-done | bytes 65552 | tf_op jit(solution)/shard_map/reduce_scatter | solution.py:116
  326.6 1.3 collective-permute-start.7
  327.9 6.3 %collective-permute-done.7 = f32[128,128]{1,0:T(8,128)S(1)} collective-permute-done((f32[128,128]{1,0:T(8,128)}, f32[128,128]{1,0:T(8,128)S(1)}, u32[]{:S(2)}, u32[]{:S(2)}) %collective-permute-start.7) | collective-permute-done | bytes 65568 | tf_op jit(solution)/shard_map/ppermute | solution.py:10
  334.1 5.8 %all_gather.31 = f32[128,512]{1,0:T(8,128)S(1)} all-gather(f32[128,128]{1,0:T(8,128)S(1)} %get-tuple-element.6), channel_id=1, replica_groups=mesh['tm'=8,'col'=4] {'col'}, dimensions={1}, use_global_device_ids=true | all-gather | bytes 327680 | tf_op jit(solution)/shard_map/all_gather | solution.py:24
  (60 shorter events, 5.3 us)
Async XLA Ops:
  7.2 2.0 copy-start.8
  7.2 3.1 copy-start.9
  7.2 3.1 copy-start.5
  7.2 23.4 %all-gather.4.cloned.1.call-start = ((), (), s32[]{:S(2)}) async-start(), calls=%async_computation.4 | async-start | bytes 1638400 | tf_op jit(solution)/shard_map/all_gather | solution.py:18
  8.1 44.3 %all-gather.6.cloned.1.call-start = ((), (), s32[]{:S(2)}) async-start(), calls=%async_computation.5 | async-start | bytes 1638400 | tf_op jit(solution)/shard_map/all_gather | solution.py:18
  33.9 40.2 %all-gather.8.cloned.1.call-start = ((), (), s32[]{:S(2)}) async-start(), calls=%async_computation.6 | async-start | bytes 1638400 | tf_op jit(solution)/shard_map/all_gather | solution.py:72
  74.1 32.1 %collective-permute-start = (f32[640,512]{1,0:T(8,128)}, f32[640,512]{1,0:T(8,128)S(1)}, u32[]{:S(2)}, u32[]{:S(2)}) collective-permute-start(f32[640,512]{1,0:T(8,128)} %all-gather.8.cloned.1.call-done), channel_id=1, source_target_pairs={{0,4},{4,8},{8,12},{12,16},{16,20},{20,24},{24,28},{1,5},{5,9},{9,... | collective-permute-start | bytes 3932168 | tf_op jit(solution)/shard_map/ppermute | solution.py:10
  110.1 32.8 %collective-permute-start.1 = (f32[640,512]{1,0:T(8,128)S(1)}, f32[640,512]{1,0:T(8,128)}, u32[]{:S(2)}, u32[]{:S(2)}) collective-permute-start(f32[640,512]{1,0:T(8,128)S(1)} %fusion), channel_id=1, source_target_pairs={{0,8},{4,12},{8,16},{12,20},{16,24},{20,28},{1,9},{5,13},{9,17},{1... | collective-permute-start | bytes 3932168 | tf_op jit(solution)/shard_map/ppermute | solution.py:10
  146.4 32.2 %collective-permute-start.2 = (f32[640,512]{1,0:T(8,128)S(1)}, f32[640,512]{1,0:T(8,128)}, u32[]{:S(2)}, u32[]{:S(2)}) collective-permute-start(f32[640,512]{1,0:T(8,128)S(1)} %fusion.1), channel_id=1, source_target_pairs={{0,16},{4,20},{8,24},{12,28},{1,17},{5,21},{9,25},{13,29},{2,18},{... | collective-permute-start | bytes 3932168 | tf_op jit(solution)/shard_map/ppermute | solution.py:10
  156.5 9.4 %all-to-all-start = ((bf16[4,2,128,128]{2,3,1,0:T(8,128)(2,1)}), bf16[4,2,128,128]{2,3,1,0:T(8,128)(2,1)S(1)}, u32[]{:S(2)}, u32[]{:S(2)}) async-start(bf16[4,2,128,128]{2,3,1,0:T(8,128)(2,1)} %pad_maximum_fusion), calls=%async_computation | async-start | bytes 524288 | tf_op jit(solution)/shard_map/all_to_all | solution.py:53
  159.9 112.2 %reduce-scatter.4.cloned.1.call-start = ((), (), s32[]{:S(2)}) async-start(), calls=%async_computation.7 | async-start | bytes 327680 | tf_op jit(solution)/shard_map/reduce_scatter | solution.py:116
  165.9 18.9 %copy-start.6 = (f32[128,512]{0,1:T(8,128)S(1)}, f32[128,512]{0,1:T(8,128)}, u32[]{:S(2)}) copy-start(f32[128,512]{0,1:T(8,128)} %fusion.15) | copy-start | bytes 786436
  166.0 18.9 %copy-start.7 = (f32[128,512]{0,1:T(8,128)S(1)}, f32[128,512]{0,1:T(8,128)}, u32[]{:S(2)}) copy-start(f32[128,512]{0,1:T(8,128)} %fusion.18) | copy-start | bytes 786436
  182.2 10.5 %copy-start = (f32[640,128]{1,0:T(8,128)S(1)}, f32[640,128]{1,0:T(8,128)}, u32[]{:S(2)}) copy-start(f32[640,128]{1,0:T(8,128)} %convolution_add_fusion.3) | copy-start | bytes 983044
  182.2 10.5 %copy-start.1 = (f32[640,128]{1,0:T(8,128)S(1)}, f32[640,128]{1,0:T(8,128)}, u32[]{:S(2)}) copy-start(f32[640,128]{1,0:T(8,128)} %convolution_add_fusion.2) | copy-start | bytes 983044
  182.2 4.5 %collective-permute-start.3 = (f32[128,128]{1,0:T(8,128)S(1)}, f32[128,128]{1,0:T(8,128)S(1)}, u32[]{:S(2)}, u32[]{:S(2)}) collective-permute-start(f32[128,128]{1,0:T(8,128)S(1)} %fusion.22), channel_id=1, source_target_pairs={{0,4},{4,8},{8,12},{12,16},{16,20},{20,24},{24,28},{1,5},{5,9},{9,... | collective-permute-start | bytes 196616 | tf_op jit(solution)/shard_map/ppermute | solution.py:10
  184.9 28.4 %copy-start.2 = (f32[2,128,512]{1,2,0:T(8,128)}, f32[2,128,512]{1,2,0:T(8,128)S(1)}, u32[]{:S(2)}) copy-start(f32[2,128,512]{1,2,0:T(8,128)S(1)} %fusion.6) | copy-start | bytes 1572868
  193.1 146.8 %copy-start.4 = (f32[2,128,128]{2,1,0:T(8,128)}, f32[2,128,128]{2,1,0:T(8,128)S(1)}, u32[]{:S(2)}) copy-start(f32[2,128,128]{2,1,0:T(8,128)S(1)} %fusion.2) | copy-start | bytes 393220
  213.7 34.9 %collective-permute-start.4 = (f32[128,128]{1,0:T(8,128)S(1)}, f32[128,128]{1,0:T(8,128)S(1)}, u32[]{:S(2)}, u32[]{:S(2)}) collective-permute-start(f32[128,128]{1,0:T(8,128)S(1)} %convolution_add_fusion.5), channel_id=1, source_target_pairs={{4,0},{8,4},{12,8},{16,12},{20,16},{24,20},{28,24},{5,1},{9,5},{13... | collective-permute-start | bytes 196616 | tf_op jit(solution)/shard_map/ppermute | solution.py:10
  249.7 50.1 %reduce-scatter.6.cloned.1.call-start = ((), (), s32[]{:S(2)}) async-start(), calls=%async_computation.8 | async-start | bytes 327680 | tf_op jit(solution)/shard_map/reduce_scatter | solution.py:116
  272.1 6.4 %collective-permute-start.5 = (f32[128,128]{1,0:T(8,128)}, f32[128,128]{1,0:T(8,128)S(1)}, u32[]{:S(2)}, u32[]{:S(2)}) collective-permute-start(f32[128,128]{1,0:T(8,128)} %reduce-scatter.4.cloned.1.call-done), channel_id=1, source_target_pairs={{4,0},{8,4},{12,8},{16,12},{20,16},{24,20},{28,24},{5,1},{9,5},{13... | collective-permute-start | bytes 196616 | tf_op jit(solution)/shard_map/ppermute | solution.py:10
  279.6 47.0 %reduce-scatter.8.cloned.1.call-start = ((), (), s32[]{:S(2)}) async-start(), calls=%async_computation.9 | async-start | bytes 327680 | tf_op jit(solution)/shard_map/reduce_scatter | solution.py:116
  299.8 6.4 %collective-permute-start.6 = (f32[128,128]{1,0:T(8,128)}, f32[128,128]{1,0:T(8,128)S(1)}, u32[]{:S(2)}, u32[]{:S(2)}) collective-permute-start(f32[128,128]{1,0:T(8,128)} %reduce-scatter.6.cloned.1.call-done), channel_id=1, source_target_pairs={{8,0},{12,4},{16,8},{20,12},{24,16},{28,20},{9,1},{13,5},{17,9},{2... | collective-permute-start | bytes 196616 | tf_op jit(solution)/shard_map/ppermute | solution.py:10
  301.2 38.7 %copy-start.3 = (f32[2,128,512]{1,2,0:T(8,128)S(1)}, f32[2,128,512]{1,2,0:T(8,128)}, u32[]{:S(2)}) copy-start(f32[2,128,512]{1,2,0:T(8,128)} %copy-done.2) | copy-start | bytes 1572868
  326.6 7.5 %collective-permute-start.7 = (f32[128,128]{1,0:T(8,128)}, f32[128,128]{1,0:T(8,128)S(1)}, u32[]{:S(2)}, u32[]{:S(2)}) collective-permute-start(f32[128,128]{1,0:T(8,128)} %reduce-scatter.8.cloned.1.call-done), channel_id=1, source_target_pairs={{16,0},{20,4},{24,8},{28,12},{17,1},{21,5},{25,9},{29,13},{18,2},{... | collective-permute-start | bytes 196616 | tf_op jit(solution)/shard_map/ppermute | solution.py:10
Sparse Core Ops, SparseCore 0:
  9.6 21.0 all-gather.3
  34.0 18.3 all-gather.5
  55.7 18.3 all-gather.7
  249.8 22.2 reduce-scatter.3
  279.7 20.0 reduce-scatter.5
  307.4 19.1 reduce-scatter.7
